TPU v7x, 32 devices: a whole 2x2x4 slice. The times are simulated.
32 devices in a mesh: ctx: 4 (over y, core), ep: 8 (over z, x).
Axes of the slice: x: 2, y: 2, z: 4, core: 2. Of those that a mesh axis runs over, the one named last changes fastest.
Arguments:
- tokens: bfloat16 [1024, 3584], P('ep', 'ctx'), may hold values from -6 to 6
- cotangent: bfloat16 [1024, 3584], P('ep', 'ctx'), may hold values from -0.8984375 to 0.8984375
- expert_ids: int32 [1024, 1], P('ep'), may hold values from 0 to 7; in each aligned block of 128 rows (0 to 127, 128 to 255, ...) at most 24 rows name the same one
- route_gates: float32 [1024, 1], P('ep'), may hold values from 0.1 to 1
- w_gate: bfloat16 [8, 3584, 2048], P('ep', None, 'ctx'), may hold values from -0.125 to 0.125
- w_up: bfloat16 [8, 3584, 2048], P('ep', None, 'ctx'), may hold values from -0.09375 to 0.09375
- w_down: bfloat16 [8, 2048, 3584], P('ep', 'ctx'), may hold values from -0.1875 to 0.1875
Outputs:
- layer_out: bfloat16 [1024, 3584], P('ep', 'ctx')
- input_grad: bfloat16 [1024, 3584], P('ep', 'ctx')
- gate_grad: float32 [1024, 1], P('ep')
- w_gate_grad: bfloat16 [8, 3584, 2048], P('ep', None, 'ctx')
- w_up_grad: bfloat16 [8, 3584, 2048], P('ep', None, 'ctx')
Inputs may be any that keep to these rules, and one draw needn't show every extreme that they name: `expert_ids`: within each aligned block of 128 tokens (the tokens of one index of ep) no expert is named more than 24 times, a bound that some block reaches; the routes of one token name different experts.
All inputs are finite; a program needn't handle non-finite values.
Results may differ from a plain program's by a relative error of at most 0.015.
Values may be sent and summed in bfloat16 or wider, within the bound.
No kernel may reach another device: no remote copies, remote signals or barrier semaphores. Data moves between devices by JAX's collectives and lax.ppermute only.
A program may use at most 128 MiB of HBM per device.

v0:
```python
import jax
import jax.numpy as jnp
from jax import lax
from jax.sharding import PartitionSpec as P


def route_onehot(expert_ids, experts, capacity):
    tok_rows, routes = expert_ids.shape
    flat_ids = expert_ids.reshape(-1)
    labels = jnp.arange(experts, dtype=jnp.int32)
    onehot = (flat_ids[:, None] == labels[None, :]).astype(jnp.bfloat16)
    pairs = jnp.arange(flat_ids.shape[0], dtype=jnp.int32)
    before = (pairs[:, None] > pairs[None, :]).astype(jnp.bfloat16)
    earlier = jnp.dot(before, onehot, preferred_element_type=jnp.float32)
    slot_rank = jnp.sum(earlier * onehot.astype(jnp.float32), axis=1).astype(jnp.int32)
    slot_ids = (flat_ids * capacity + slot_rank).reshape(tok_rows, routes)
    positions = jnp.arange(experts * capacity, dtype=jnp.int32)
    return [slot_ids[:, r][:, None] == positions[None, :] for r in range(routes)]


def split_f32(values):
    hi = values.astype(jnp.bfloat16)
    lo = (values - hi.astype(jnp.float32)).astype(jnp.bfloat16)
    return (hi, lo)


def join_f32(hi, lo):
    return hi.astype(jnp.float32) + lo.astype(jnp.float32)


def ctx_bits(n_ctx):
    bits = n_ctx.bit_length() - 1
    assert 1 << bits == n_ctx
    return bits


def xor_pairs(n_ctx, bit):
    return [(i, i ^ 1 << bit) for i in range(n_ctx)]


def gather_blocks(block, n_ctx, me):
    held = block[None]
    for bit in reversed(range(ctx_bits(n_ctx))):
        other = lax.ppermute(held, "ctx", xor_pairs(n_ctx, bit))
        mine_first = me >> bit & 1 == 0
        pair = jnp.where(
            mine_first, jnp.stack([held, other], axis=1), jnp.stack([other, held], axis=1)
        )
        held = pair.reshape((-1,) + block.shape)
    return held


def scatter_sum(blocks, n_ctx, me):
    acc = blocks
    for bit in range(ctx_bits(n_ctx)):
        halves = acc.reshape((-1, 2) + acc.shape[1:])
        keep_first = me >> bit & 1 == 0
        keep = jnp.where(keep_first, halves[:, 0], halves[:, 1])
        send = jnp.where(keep_first, halves[:, 1], halves[:, 0]).astype(jnp.bfloat16)
        got = lax.ppermute(send, "ctx", xor_pairs(n_ctx, bit))
        acc = keep + got.astype(jnp.float32)
    return acc[0]


def all_sum(values, n_ctx):
    for bit in range(ctx_bits(n_ctx)):
        values = values + lax.ppermute(values, "ctx", xor_pairs(n_ctx, bit))
    return values


def with_cols(rows, values, pad):
    hi, lo = split_f32(values)
    zeros = jnp.zeros((rows.shape[0], pad - 2), jnp.bfloat16)
    return jnp.concatenate([rows, hi[:, None], lo[:, None], zeros], axis=1)


def shards(tokens, cotangent, expert_ids, route_gates, w_gate, w_up, w_down):
    tok_rows, routes = expert_ids.shape
    experts = lax.axis_size("ep")
    n_ctx = lax.axis_size("ctx")
    me = lax.axis_index("ctx")
    capacity = 3 * tok_rows * routes // (2 * experts)
    slot_count = experts * capacity
    col_width = tokens.shape[1]
    pad = 128
    route_maps = route_onehot(expert_ids, experts, capacity)

    def place(values):
        placed = jnp.zeros((slot_count, values.shape[1]), jnp.float32)
        for chosen in route_maps:
            placed = placed + jnp.einsum(
                "ts,tc->sc", chosen.astype(jnp.bfloat16), values, preferred_element_type=jnp.float32
            )
        return placed.astype(jnp.bfloat16)

    def to_experts(rows):
        sent = rows.reshape(experts, capacity, rows.shape[1])
        got = lax.all_to_all(sent, "ep", split_axis=0, concat_axis=0, tiled=True)
        return got.reshape(slot_count, rows.shape[1])

    slot_gates = jnp.zeros((slot_count,), jnp.float32)
    for r, chosen in enumerate(route_maps):
        slot_gates = slot_gates + jnp.sum(
            jnp.where(chosen, route_gates[:, r][:, None], 0.0), axis=0
        )
    got_x = to_experts(with_cols(place(tokens), slot_gates, pad))
    gate_column = join_f32(got_x[:, col_width], got_x[:, col_width + 1])[:, None]
    rows_in = gather_blocks(got_x[:, :col_width], n_ctx, me)
    got_dy = to_experts(place(cotangent))
    grads_in = gather_blocks(got_dy, n_ctx, me)
    group = w_gate.shape[2]
    gate_w = w_gate[0].reshape(n_ctx, col_width, group)
    up_w = w_up[0].reshape(n_ctx, col_width, group)
    down_w = w_down[0]
    down_cols = [down_w[:, q * col_width : (q + 1) * col_width] for q in range(n_ctx)]
    pre_gate = jnp.einsum("nsd,ndf->sf", rows_in, gate_w, preferred_element_type=jnp.float32)
    pre_up = jnp.einsum("nsd,ndf->sf", rows_in, up_w, preferred_element_type=jnp.float32)
    sigma = jax.nn.sigmoid(pre_gate)
    activated = pre_gate * sigma
    hidden = (activated * pre_up).astype(jnp.bfloat16)
    partial_out = jnp.stack(
        [jnp.dot(hidden, cols, preferred_element_type=jnp.float32) for cols in down_cols]
    ).astype(jnp.bfloat16)
    gate_part = jnp.einsum(
        "nsd,nsd->s", partial_out.astype(jnp.float32), grads_in.astype(jnp.float32)
    )
    expert_out = scatter_sum(partial_out.astype(jnp.float32), n_ctx, me).astype(jnp.bfloat16)
    gate_sum = all_sum(gate_part, n_ctx)
    back_out = to_experts(with_cols(expert_out, gate_sum, pad))
    contract_last = (((1,), (1,)), ((), ()))
    down_t = sum(
        (
            lax.dot_general(
                grads_in[q], down_cols[q], contract_last, preferred_element_type=jnp.float32
            )
            for q in range(n_ctx)
        )
    )
    hidden_grad = gate_column * down_t
    grad_gate = (hidden_grad * pre_up * sigma * (1.0 + pre_gate * (1.0 - sigma))).astype(
        jnp.bfloat16
    )
    grad_up = (hidden_grad * activated).astype(jnp.bfloat16)
    back_terms = jnp.einsum(
        "sf,ndf->nsd", grad_gate, gate_w, preferred_element_type=jnp.float32
    ) + jnp.einsum("sf,ndf->nsd", grad_up, up_w, preferred_element_type=jnp.float32)
    back_terms = back_terms.astype(jnp.bfloat16).astype(jnp.float32)
    slot_grad = scatter_sum(back_terms, n_ctx, me).astype(jnp.bfloat16)
    back_grad = to_experts(slot_grad)
    w_gate_grad = (
        jnp.einsum("nsd,sf->ndf", rows_in, grad_gate, preferred_element_type=jnp.float32)
        .astype(jnp.bfloat16)
        .reshape(1, n_ctx * col_width, group)
    )
    w_up_grad = (
        jnp.einsum("nsd,sf->ndf", rows_in, grad_up, preferred_element_type=jnp.float32)
        .astype(jnp.bfloat16)
        .reshape(1, n_ctx * col_width, group)
    )
    layer_out = jnp.zeros((tok_rows, col_width), jnp.float32)
    input_grad = jnp.zeros((tok_rows, col_width), jnp.float32)
    gate_terms = []
    for r, chosen in enumerate(route_maps):
        pick = chosen.astype(jnp.bfloat16)
        rows_r = jnp.dot(pick, back_out, preferred_element_type=jnp.float32)
        layer_out = layer_out + route_gates[:, r][:, None] * rows_r[:, :col_width]
        input_grad = input_grad + jnp.dot(pick, back_grad, preferred_element_type=jnp.float32)
        gate_terms.append(rows_r[:, col_width] + rows_r[:, col_width + 1])
    gate_grad = jnp.stack(gate_terms, axis=1)
    return (
        layer_out.astype(jnp.bfloat16),
        input_grad.astype(jnp.bfloat16),
        gate_grad,
        w_gate_grad,
        w_up_grad,
    )


def solution(mesh):
    in_specs = (
        P("ep", "ctx"),
        P("ep", "ctx"),
        P("ep", None),
        P("ep", None),
        P("ep", None, "ctx"),
        P("ep", None, "ctx"),
        P("ep", "ctx", None),
    )
    out_specs = (
        P("ep", "ctx"),
        P("ep", "ctx"),
        P("ep", None),
        P("ep", None, "ctx"),
        P("ep", None, "ctx"),
    )
    return jax.shard_map(shards, mesh=mesh, in_specs=in_specs, out_specs=out_specs, check_vma=False)
```

profile of v0, /device:TPU:0, one launch (start us, length us, event | category | flops | bytes accessed | tf_op | source)
XLA Modules:
  0.0 105.1 jit_solution(2697727353516576229)
XLA Ops:
  3.2 7.3 %all-to-all-start.1 = ((bf16[8,24,896]{2,1,0:T(8,128)(2,1)}), bf16[8,24,896]{2,1,0:T(8,128)(2,1)S(1)}, u32[]{:S(2)}, u32[]{:S(2)}) async-start(bf16[8,24,896]{2,1,0:T(8,128)(2,1)} %bitcast.34), calls=%async_computation.1 | async-start | bytes 688128 | tf_op jit(solution)/shard_map/all_to_all | solution.py:98
  12.8 8.3 %all-to-all-done.1 = bf16[8,24,896]{2,1,0:T(8,128)(2,1)S(1)} async-done(((bf16[8,24,896]{2,1,0:T(8,128)(2,1)}), bf16[8,24,896]{2,1,0:T(8,128)(2,1)S(1)}, u32[]{:S(2)}, u32[]{:S(2)}) %all-to-all-start.1) | async-done | bytes 344096 | tf_op jit(solution)/shard_map/all_to_all | solution.py:98
  21.1 3.6 %all-to-all-start = ((bf16[8,24,1024]{2,1,0:T(8,128)(2,1)}), bf16[8,24,1024]{2,1,0:T(8,128)(2,1)S(1)}, u32[]{:S(2)}, u32[]{:S(2)}) async-start(bf16[8,24,1024]{2,1,0:T(8,128)(2,1)} %maximum_maximum_fusion), calls=%async_computation | async-start | bytes 786432 | tf_op jit(solution)/shard_map/all_to_all | solution.py:98
  24.7 1.5 %collective-permute-start.4 = (bf16[1,192,896]{2,1,0:T(8,128)(2,1)S(1)}, bf16[1,192,896]{2,1,0:T(8,128)(2,1)S(1)}, u32[]{:S(2)}, u32[]{:S(2)}) collective-permute-start(bf16[1,192,896]{2,1,0:T(8,128)(2,1)S(1)} %bitcast.174), channel_id=1, source_target_pairs={{0,16},{8,24},{16,0},{24,8},{1,17},{9,25},{17,1},{25,9},{2,18},{10... | collective-permute-start | bytes 1032200 | tf_op jit(solution)/shard_map/ppermute | solution.py:44
  26.2 7.5 %collective-permute-done.4 = bf16[1,192,896]{2,1,0:T(8,128)(2,1)S(1)} collective-permute-done((bf16[1,192,896]{2,1,0:T(8,128)(2,1)S(1)}, bf16[1,192,896]{2,1,0:T(8,128)(2,1)S(1)}, u32[]{:S(2)}, u32[]{:S(2)}) %collective-permute-start.4) | collective-permute-done | bytes 344096 | tf_op jit(solution)/shard_map/ppermute | solution.py:44
  34.7 1.2 %all-to-all-done = bf16[8,24,1024]{2,1,0:T(8,128)(2,1)S(1)} async-done(((bf16[8,24,1024]{2,1,0:T(8,128)(2,1)}), bf16[8,24,1024]{2,1,0:T(8,128)(2,1)S(1)}, u32[]{:S(2)}, u32[]{:S(2)}) %all-to-all-start) | async-done | bytes 393248 | tf_op jit(solution)/shard_map/all_to_all | solution.py:98
  36.0 1.6 %collective-permute-start = (bf16[1,192,896]{2,1,0:T(8,128)(2,1)S(1)}, bf16[1,192,896]{2,1,0:T(8,128)(2,1)S(1)}, u32[]{:S(2)}, u32[]{:S(2)}) collective-permute-start(bf16[1,192,896]{2,1,0:T(8,128)(2,1)S(1)} %get-tuple-element.33), channel_id=1, source_target_pairs={{0,16},{8,24},{16,0},{24,8},{1,17},{9,25},{17,1},{25,9},{2,18},{10... | collective-permute-start | bytes 1032200 | tf_op jit(solution)/shard_map/ppermute | solution.py:44
  37.9 7.4 %collective-permute-done = bf16[1,192,896]{2,1,0:T(8,128)(2,1)S(1)} collective-permute-done((bf16[1,192,896]{2,1,0:T(8,128)(2,1)S(1)}, bf16[1,192,896]{2,1,0:T(8,128)(2,1)S(1)}, u32[]{:S(2)}, u32[]{:S(2)}) %collective-permute-start) | collective-permute-done | bytes 344096 | tf_op jit(solution)/shard_map/ppermute | solution.py:44
  46.1 1.6 %copy-done.3 = bf16[1,512,3584]{2,1,0:T(8,128)(2,1)S(1)} copy-done((bf16[1,512,3584]{2,1,0:T(8,128)(2,1)S(1)}, bf16[1,512,3584]{2,1,0:T(8,128)(2,1)}, u32[]{:S(2)}) %copy-start.3) | copy-done | bytes 3670040
  49.4 1.3 %copy-done.2 = bf16[1,3584,512]{2,1,0:T(8,128)(2,1)S(1)} copy-done((bf16[1,3584,512]{2,1,0:T(8,128)(2,1)S(1)}, bf16[1,3584,512]{2,1,0:T(8,128)(2,1)}, u32[]{:S(2)}) %copy-start.2) | copy-done | bytes 3670040
  51.6 1.2 %copy-done.1 = bf16[1,3584,512]{2,1,0:T(8,128)(2,1)S(1)} copy-done((bf16[1,3584,512]{2,1,0:T(8,128)(2,1)S(1)}, bf16[1,3584,512]{2,1,0:T(8,128)(2,1)}, u32[]{:S(2)}) %copy-start.1) | copy-done | bytes 3670040
  55.7 1.3 %fusion.27 = f32[192,4,896]{2,0,1:T(8,128)S(1)} fusion(bf16[4,896,512]{2,1,0:T(8,128)(2,1)S(1)} %bitcast.169, bf16[192,512]{1,0:T(8,128)(2,1)S(1)} %get-tuple-element.30), kind=kOutput, calls=%fused_computation.74 | convolution fusion | flops 704643072 | bytes 6619136 | tf_op jit(solution)/shard_map/sf,ndf->nsd/dot_general | solution.py:144
  57.1 1.3 %fusion.1 = f32[192,4,896]{2,0,1:T(8,128)S(1)} fusion(f32[192,4,896]{2,0,1:T(8,128)S(1)} %fusion.27, bf16[192,512,1]{1,0,2:T(8,128)(2,1)S(1)} %get-tuple-element.29, bf16[4,896,512]{2,1,0:T(8,128)(2,1)S(1)} %bitcast.171), kind=kOutput, calls=%fused_computation.6 | convolution fusion | flops 706707456 | bytes 9371648 | tf_op jit(solution)/shard_map/sf,ndf->nsd/dot_general | solution.py:146
  60.5 1.6 %collective-permute-done.6 = f32[192]{0:T(256)S(1)} collective-permute-done((f32[192]{0:T(256)S(1)}, f32[192]{0:T(256)S(1)}, u32[]{:S(2)}, u32[]{:S(2)}) %collective-permute-start.6) | collective-permute-done | bytes 800 | tf_op jit(solution)/shard_map/ppermute | solution.py:67
  62.2 1.5 %collective-permute-start.7 = (f32[192]{0:T(256)S(1)}, f32[192]{0:T(256)S(1)}, u32[]{:S(2)}, u32[]{:S(2)}) collective-permute-start(f32[192]{0:T(256)S(1)} %add.53), channel_id=1, source_target_pairs={{0,16},{8,24},{16,0},{24,8},{1,17},{9,25},{17,1},{25,9},{2,18},{10... | collective-permute-start | bytes 2312 | tf_op jit(solution)/shard_map/ppermute | solution.py:67
  65.5 1.5 %collective-permute-start.3 = (bf16[1,192,896]{2,1,0:T(8,128)(2,1)}, bf16[1,192,896]{2,1,0:T(8,128)(2,1)}, u32[]{:S(2)}, u32[]{:S(2)}) collective-permute-start(bf16[1,192,896]{2,1,0:T(8,128)(2,1)} %fusion.23), channel_id=1, source_target_pairs={{0,16},{8,24},{16,0},{24,8},{1,17},{9,25},{17,1},{25,9},{2,18},{10... | collective-permute-start | bytes 1032200 | tf_op jit(solution)/shard_map/ppermute | solution.py:60
  67.0 7.9 %collective-permute-done.9 = bf16[1,192,896]{2,1,0:T(8,128)(2,1)S(1)} collective-permute-done((bf16[1,192,896]{2,1,0:T(8,128)(2,1)S(1)}, bf16[1,192,896]{2,1,0:T(8,128)(2,1)S(1)}, u32[]{:S(2)}, u32[]{:S(2)}) %collective-permute-start.9) | collective-permute-done | bytes 344096 | tf_op jit(solution)/shard_map/ppermute | solution.py:60
  75.8 5.7 %all-to-all-start.3 = ((bf16[8,24,896]{2,1,0:T(8,128)(2,1)}), bf16[8,24,896]{2,1,0:T(8,128)(2,1)S(1)}, u32[]{:S(2)}, u32[]{:S(2)}) async-start(bf16[8,24,896]{2,1,0:T(8,128)(2,1)} %bitcast.185), calls=%async_computation.3 | async-start | bytes 688128 | tf_op jit(solution)/shard_map/all_to_all | solution.py:98
  83.2 1.1 %fusion.20 = bf16[1,192,896]{2,1,0:T(8,128)(2,1)S(1)} fusion(bf16[1,192,896]{2,1,0:T(8,128)(2,1)} %collective-permute-done.3, f32[1,2,192,896]{3,2,1,0:T(8,128)S(1)} %fusion.4, pred[]{:T(512)S(6)} %eq.50), kind=kLoop, calls=%fused_computation.52 | loop fusion | flops 688128 | bytes 2064385 | tf_op jit(solution)/shard_map/convert_element_type | solution.py:127
  85.2 5.2 %all-to-all-done.3 = bf16[8,24,896]{2,1,0:T(8,128)(2,1)S(1)} async-done(((bf16[8,24,896]{2,1,0:T(8,128)(2,1)}), bf16[8,24,896]{2,1,0:T(8,128)(2,1)S(1)}, u32[]{:S(2)}, u32[]{:S(2)}) %all-to-all-start.3) | async-done | bytes 344096 | tf_op jit(solution)/shard_map/all_to_all | solution.py:98
  90.3 3.6 %all-to-all-start.2 = ((bf16[8,24,1024]{2,1,0:T(8,128)(2,1)}), bf16[8,24,1024]{2,1,0:T(8,128)(2,1)S(1)}, u32[]{:S(2)}, u32[]{:S(2)}) async-start(bf16[8,24,1024]{2,1,0:T(8,128)(2,1)} %maximum_maximum_fusion.1), calls=%async_computation.2 | async-start | bytes 786432 | tf_op jit(solution)/shard_map/all_to_all | solution.py:98
  94.0 3.0 %convolution_convert_fusion = bf16[4,896,512]{2,1,0:T(8,128)(2,1)} fusion(bf16[4,192,896]{2,1,0:T(8,128)(2,1)S(1)} %bitcast.160, bf16[192,512,1]{1,0,2:T(8,128)(2,1)S(1)} %copy-done.5), kind=kOutput, calls=%fused_computation.4 | convolution fusion | flops 706478080 | bytes 5242880 | tf_op jit(solution)/shard_map/nsd,sf->ndf/dot_general | solution.py:156
  97.0 3.0 %convolution_convert_fusion.1 = bf16[4,896,512]{2,1,0:T(8,128)(2,1)} fusion(bf16[4,192,896]{2,1,0:T(8,128)(2,1)S(1)} %bitcast.161, bf16[192,512]{1,0:T(8,128)(2,1)S(1)} %get-tuple-element.30), kind=kOutput, calls=%fused_computation.5 | convolution fusion | flops 706478080 | bytes 5242880 | tf_op jit(solution)/shard_map/nsd,sf->ndf/dot_general | solution.py:151
  101.0 2.4 %all-to-all-done.2 = bf16[8,24,1024]{2,1,0:T(8,128)(2,1)S(1)} async-done(((bf16[8,24,1024]{2,1,0:T(8,128)(2,1)}), bf16[8,24,1024]{2,1,0:T(8,128)(2,1)S(1)}, u32[]{:S(2)}, u32[]{:S(2)}) %all-to-all-start.2) | async-done | bytes 393248 | tf_op jit(solution)/shard_map/all_to_all | solution.py:98
  (79 shorter events, 22.3 us)
Async XLA Ops:
  0.6 1.6 %copy-start = (bf16[128,896]{1,0:T(8,128)(2,1)S(1)}, bf16[128,896]{1,0:T(8,128)(2,1)}, u32[]{:S(2)}) copy-start(bf16[128,896]{1,0:T(8,128)(2,1)} %param.8) | copy-start | bytes 688132
  0.6 11.0 %copy-start.6 = (bf16[128,896]{1,0:T(8,128)(2,1)S(1)}, bf16[128,896]{1,0:T(8,128)(2,1)}, u32[]{:S(2)}) copy-start(bf16[128,896]{1,0:T(8,128)(2,1)} %param.7) | copy-start | bytes 688132
  3.2 17.9 %all-to-all-start.1 = ((bf16[8,24,896]{2,1,0:T(8,128)(2,1)}), bf16[8,24,896]{2,1,0:T(8,128)(2,1)S(1)}, u32[]{:S(2)}, u32[]{:S(2)}) async-start(bf16[8,24,896]{2,1,0:T(8,128)(2,1)} %bitcast.34), calls=%async_computation.1 | async-start | bytes 688128 | tf_op jit(solution)/shard_map/all_to_all | solution.py:98
  21.1 14.9 %all-to-all-start = ((bf16[8,24,1024]{2,1,0:T(8,128)(2,1)}), bf16[8,24,1024]{2,1,0:T(8,128)(2,1)S(1)}, u32[]{:S(2)}, u32[]{:S(2)}) async-start(bf16[8,24,1024]{2,1,0:T(8,128)(2,1)} %maximum_maximum_fusion), calls=%async_computation | async-start | bytes 786432 | tf_op jit(solution)/shard_map/all_to_all | solution.py:98
  24.7 9.1 %collective-permute-start.4 = (bf16[1,192,896]{2,1,0:T(8,128)(2,1)S(1)}, bf16[1,192,896]{2,1,0:T(8,128)(2,1)S(1)}, u32[]{:S(2)}, u32[]{:S(2)}) collective-permute-start(bf16[1,192,896]{2,1,0:T(8,128)(2,1)S(1)} %bitcast.174), channel_id=1, source_target_pairs={{0,16},{8,24},{16,0},{24,8},{1,17},{9,25},{17,1},{25,9},{2,18},{10... | collective-permute-start | bytes 1032200 | tf_op jit(solution)/shard_map/ppermute | solution.py:44
  34.7 10.9 %collective-permute-start.5 = (bf16[2,192,896]{2,1,0:T(8,128)(2,1)}, bf16[2,192,896]{2,1,0:T(8,128)(2,1)S(1)}, u32[]{:S(2)}, u32[]{:S(2)}) collective-permute-start(bf16[2,192,896]{2,1,0:T(8,128)(2,1)} %maximum_select_fusion.4), channel_id=1, source_target_pairs={{0,8},{8,0},{16,24},{24,16},{1,9},{9,1},{17,25},{25,17},{2,10},{10... | collective-permute-start | bytes 2064392 | tf_op jit(solution)/shard_map/ppermute | solution.py:44
  36.0 9.3 %collective-permute-start = (bf16[1,192,896]{2,1,0:T(8,128)(2,1)S(1)}, bf16[1,192,896]{2,1,0:T(8,128)(2,1)S(1)}, u32[]{:S(2)}, u32[]{:S(2)}) collective-permute-start(bf16[1,192,896]{2,1,0:T(8,128)(2,1)S(1)} %get-tuple-element.33), channel_id=1, source_target_pairs={{0,16},{8,24},{16,0},{24,8},{1,17},{9,25},{17,1},{25,9},{2,18},{10... | collective-permute-start | bytes 1032200 | tf_op jit(solution)/shard_map/ppermute | solution.py:44
  45.5 3.7 %collective-permute-start.1 = (bf16[2,192,896]{2,1,0:T(8,128)(2,1)S(1)}, bf16[2,192,896]{2,1,0:T(8,128)(2,1)S(1)}, u32[]{:S(2)}, u32[]{:S(2)}) collective-permute-start(bf16[2,192,896]{2,1,0:T(8,128)(2,1)S(1)} %maximum_select_fusion.2), channel_id=1, source_target_pairs={{0,8},{8,0},{16,24},{24,16},{1,9},{9,1},{17,25},{25,17},{2,10},{10... | collective-permute-start | bytes 2064392 | tf_op jit(solution)/shard_map/ppermute | solution.py:44
  45.7 2.0 %copy-start.3 = (bf16[1,512,3584]{2,1,0:T(8,128)(2,1)S(1)}, bf16[1,512,3584]{2,1,0:T(8,128)(2,1)}, u32[]{:S(2)}) copy-start(bf16[1,512,3584]{2,1,0:T(8,128)(2,1)} %param.13) | copy-start | bytes 11010052
  48.7 2.0 %copy-start.2 = (bf16[1,3584,512]{2,1,0:T(8,128)(2,1)S(1)}, bf16[1,3584,512]{2,1,0:T(8,128)(2,1)}, u32[]{:S(2)}) copy-start(bf16[1,3584,512]{2,1,0:T(8,128)(2,1)} %param.12) | copy-start | bytes 11010052
  50.7 2.0 %copy-start.1 = (bf16[1,3584,512]{2,1,0:T(8,128)(2,1)S(1)}, bf16[1,3584,512]{2,1,0:T(8,128)(2,1)}, u32[]{:S(2)}) copy-start(bf16[1,3584,512]{2,1,0:T(8,128)(2,1)} %param.11) | copy-start | bytes 11010052
  54.2 2.9 %copy-start.4 = (bf16[192,512,1]{1,0,2:T(8,128)(2,1)}, bf16[192,512,1]{1,0,2:T(8,128)(2,1)S(1)}, u32[]{:S(2)}) copy-start(bf16[192,512,1]{1,0,2:T(8,128)(2,1)S(1)} %get-tuple-element.29) | copy-start | bytes 589828
  58.6 5.1 %collective-permute-start.8 = (bf16[2,192,896]{2,1,0:T(8,128)(2,1)S(1)}, bf16[2,192,896]{2,1,0:T(8,128)(2,1)S(1)}, u32[]{:S(2)}, u32[]{:S(2)}) collective-permute-start(bf16[2,192,896]{2,1,0:T(8,128)(2,1)S(1)} %fusion.18), channel_id=1, source_target_pairs={{0,8},{8,0},{16,24},{24,16},{1,9},{9,1},{17,25},{25,17},{2,10},{10... | collective-permute-start | bytes 2064392 | tf_op jit(solution)/shard_map/ppermute | solution.py:60
  59.9 4.6 %collective-permute-start.2 = (bf16[2,192,896]{2,1,0:T(8,128)(2,1)S(1)}, bf16[2,192,896]{2,1,0:T(8,128)(2,1)S(1)}, u32[]{:S(2)}, u32[]{:S(2)}) collective-permute-start(bf16[2,192,896]{2,1,0:T(8,128)(2,1)S(1)} %fusion.17), channel_id=1, source_target_pairs={{0,8},{8,0},{16,24},{24,16},{1,9},{9,1},{17,25},{25,17},{2,10},{10... | collective-permute-start | bytes 2064392 | tf_op jit(solution)/shard_map/ppermute | solution.py:60
  60.0 2.1 %collective-permute-start.6 = (f32[192]{0:T(256)S(1)}, f32[192]{0:T(256)S(1)}, u32[]{:S(2)}, u32[]{:S(2)}) collective-permute-start(f32[192]{0:T(256)S(1)} %get-tuple-element.25), channel_id=1, source_target_pairs={{0,8},{8,0},{16,24},{24,16},{1,9},{9,1},{17,25},{25,17},{2,10},{10... | collective-permute-start | bytes 2312 | tf_op jit(solution)/shard_map/ppermute | solution.py:67
  62.2 19.3 %collective-permute-start.7 = (f32[192]{0:T(256)S(1)}, f32[192]{0:T(256)S(1)}, u32[]{:S(2)}, u32[]{:S(2)}) collective-permute-start(f32[192]{0:T(256)S(1)} %add.53), channel_id=1, source_target_pairs={{0,16},{8,24},{16,0},{24,8},{1,17},{9,25},{17,1},{25,9},{2,18},{10... | collective-permute-start | bytes 2312 | tf_op jit(solution)/shard_map/ppermute | solution.py:67
  63.9 11.0 %collective-permute-start.9 = (bf16[1,192,896]{2,1,0:T(8,128)(2,1)S(1)}, bf16[1,192,896]{2,1,0:T(8,128)(2,1)S(1)}, u32[]{:S(2)}, u32[]{:S(2)}) collective-permute-start(bf16[1,192,896]{2,1,0:T(8,128)(2,1)S(1)} %fusion.24), channel_id=1, source_target_pairs={{0,16},{8,24},{16,0},{24,8},{1,17},{9,25},{17,1},{25,9},{2,18},{10... | collective-permute-start | bytes 1032200 | tf_op jit(solution)/shard_map/ppermute | solution.py:60
  65.5 17.7 %collective-permute-start.3 = (bf16[1,192,896]{2,1,0:T(8,128)(2,1)}, bf16[1,192,896]{2,1,0:T(8,128)(2,1)}, u32[]{:S(2)}, u32[]{:S(2)}) collective-permute-start(bf16[1,192,896]{2,1,0:T(8,128)(2,1)} %fusion.23), channel_id=1, source_target_pairs={{0,16},{8,24},{16,0},{24,8},{1,17},{9,25},{17,1},{25,9},{2,18},{10... | collective-permute-start | bytes 1032200 | tf_op jit(solution)/shard_map/ppermute | solution.py:60
  75.8 14.6 %all-to-all-start.3 = ((bf16[8,24,896]{2,1,0:T(8,128)(2,1)}), bf16[8,24,896]{2,1,0:T(8,128)(2,1)S(1)}, u32[]{:S(2)}, u32[]{:S(2)}) async-start(bf16[8,24,896]{2,1,0:T(8,128)(2,1)} %bitcast.185), calls=%async_computation.3 | async-start | bytes 688128 | tf_op jit(solution)/shard_map/all_to_all | solution.py:98
  83.2 1.1 %copy-start.7 = (bf16[8,24,1]{2,1,0:T(8,128)(2,1)S(1)}, bf16[8,24,1]{2,1,0:T(8,128)(2,1)}, u32[]{:S(2)}) copy-start(bf16[8,24,1]{2,1,0:T(8,128)(2,1)} %concatenate.62) | copy-start | bytes 1156
  83.2 1.1 %copy-start.8 = (bf16[8,24,1]{2,1,0:T(8,128)(2,1)S(1)}, bf16[8,24,1]{2,1,0:T(8,128)(2,1)}, u32[]{:S(2)}) copy-start(bf16[8,24,1]{2,1,0:T(8,128)(2,1)} %concatenate.63) | copy-start | bytes 1156
  84.3 9.7 %copy-start.5 = (bf16[192,512,1]{1,0,2:T(8,128)(2,1)S(1)}, bf16[192,512,1]{1,0,2:T(8,128)(2,1)}, u32[]{:S(2)}) copy-start(bf16[192,512,1]{1,0,2:T(8,128)(2,1)} %copy-done.4) | copy-start | bytes 589828
  90.3 13.0 %all-to-all-start.2 = ((bf16[8,24,1024]{2,1,0:T(8,128)(2,1)}), bf16[8,24,1024]{2,1,0:T(8,128)(2,1)S(1)}, u32[]{:S(2)}, u32[]{:S(2)}) async-start(bf16[8,24,1024]{2,1,0:T(8,128)(2,1)} %maximum_maximum_fusion.1), calls=%async_computation.2 | async-start | bytes 786432 | tf_op jit(solution)/shard_map/all_to_all | solution.py:98
  100.0 3.7 %copy-start.9 = (f32[128,1]{0,1:T(1,128)S(1)}, f32[128,1]{0,1:T(1,128)}, u32[]{:S(2)}) copy-start(f32[128,1]{0,1:T(1,128)} %param.10) | copy-start | bytes 1540
where the time goes:
time: 106 us; the launch traced here: 105 us
  waiting for transfers between devices  41.7 us (39%)
  starting transfers between devices  28.1 us (27%)
  matrix products  17.2 us (16%)
  other arithmetic  10.1 us (10%)
  local copies, waits for them, and re-layouts  7.04 us (7%)
    all_to_all x4, starting transfers between devices, to_experts(): got = lax.all_to_all(sent, 'ep', split_axis=0, concat_axis=0, tiled=True)  20.2 us
    all_to_all x4, waiting for transfers between devices, to_experts(): got = lax.all_to_all(sent, 'ep', split_axis=0, concat_axis=0, tiled=True)  17.1 us
    ppermute x4, waiting for transfers between devices, gather_blocks(): other = lax.ppermute(held, 'ctx', xor_pairs(n_ctx, bit))  15 us
    ppermute x4, waiting for transfers between devices, scatter_sum(): got = lax.ppermute(send, 'ctx', xor_pairs(n_ctx, bit))  7.95 us
    unnamed x21, local copies, waits for them, and re-layouts  4.71 us
    ppermute x4, starting transfers between devices, gather_blocks(): other = lax.ppermute(held, 'ctx', xor_pairs(n_ctx, bit))  3.18 us
    dot_general x1, matrix products, shards(): jnp.einsum('nsd,sf->ndf', rows_in, grad_up, preferred_element_type=jnp.fl...  3 us
    dot_general x1, matrix products, shards(): jnp.einsum('nsd,sf->ndf', rows_in, grad_gate, preferred_element_type=jnp....  3 us
  transfers between devices with their start and end apart: 14, of which 8 were waited for; matrix products, arithmetic and copies ran while one was open for 18% of the time, Pallas kernels for 0%

commit v1 on v0

--- a/solution.py
+++ b/solution.py
@@ -95,7 +95,22 @@
 
     def to_experts(rows):
         sent = rows.reshape(experts, capacity, rows.shape[1])
-        got = lax.all_to_all(sent, "ep", split_axis=0, concat_axis=0, tiled=True)
+        top, wide_out = (lax.axis_size("ep"), lax.axis_index("ep"))
+        a_now = sent.shape[0] // top
+        carry_out = list(sent.shape)
+        carry_out[0] = a_now
+        state_now = carry_out[0]
+        carry_out[0] = state_now * top
+        got = jnp.zeros(carry_out, sent.dtype)
+        tick = 0
+        while tick < top:
+            back = lax.dynamic_slice_in_dim(sent, (wide_out ^ tick) * a_now, a_now, axis=0)
+            if tick:
+                back = lax.ppermute(
+                    back, axis_name="ep", perm=tuple(((d, d ^ tick) for d in range(top)))
+                )
+            got = lax.dynamic_update_slice_in_dim(got, back, (wide_out ^ tick) * state_now, axis=0)
+            tick += 1
         return got.reshape(slot_count, rows.shape[1])
 
     slot_gates = jnp.zeros((slot_count,), jnp.float32)

time: 106 us -> 168 us (1.58)
  waiting for transfers between devices: 41.7 us -> 74.7 us
  starting transfers between devices: 28.1 us -> 58.9 us
    ppermute x0 -> x28, starting transfers between devices: none -> 50.9 us  [to_experts(): lax.ppermute(back, axis_name='ep', perm=tuple(((d, d ^ tick) for d in ran...]
    ppermute x0 -> x28, waiting for transfers between devices: none -> 48.3 us  [to_experts(): lax.ppermute(back, axis_name='ep', perm=tuple(((d, d ^ tick) for d in ran...]
    all_to_all x4 -> x0, starting transfers between devices: 20.2 us -> none  [to_experts(): got = lax.all_to_all(sent, 'ep', split_axis=0, concat_axis=0, tiled=True)]
    all_to_all x4 -> x0, waiting for transfers between devices: 17.1 us -> none  [to_experts(): got = lax.all_to_all(sent, 'ep', split_axis=0, concat_axis=0, tiled=True)]
    ppermute x4, waiting for transfers between devices: 7.95 us -> 11.6 us  [scatter_sum(): got = lax.ppermute(send, 'ctx', xor_pairs(n_ctx, bit))]
    reshape x2, other arithmetic: 0.34 us -> 2.76 us  [scatter_sum(): halves = acc.reshape((-1, 2) + acc.shape[1:])]
    unnamed x21 -> x17, local copies, waits for them, and re-layouts: 4.71 us -> 4.7 us
  transfers between devices with their start and end apart: 14 -> 38, of which waited for: 8 -> 20; matrix products, arithmetic and copies ran while one was open for 18% -> 12% of each run, Pallas kernels for 0% -> 0%
where the time goes in v1:
time: 168 us; the launch traced here: 167 us
  waiting for transfers between devices  74.7 us (44%)
  starting transfers between devices  58.9 us (35%)
  matrix products  16.5 us (10%)
  other arithmetic  9.67 us (6%)
  local copies, waits for them, and re-layouts  6.4 us (4%)
    ppermute x28, starting transfers between devices, to_experts(): lax.ppermute(back, axis_name='ep', perm=tuple(((d, d ^ tick) for d in ran...  50.9 us
    ppermute x28, waiting for transfers between devices, to_experts(): lax.ppermute(back, axis_name='ep', perm=tuple(((d, d ^ tick) for d in ran...  48.3 us
    ppermute x4, waiting for transfers between devices, gather_blocks(): other = lax.ppermute(held, 'ctx', xor_pairs(n_ctx, bit))  14.2 us
    ppermute x4, waiting for transfers between devices, scatter_sum(): got = lax.ppermute(send, 'ctx', xor_pairs(n_ctx, bit))  11.6 us
    unnamed x17, local copies, waits for them, and re-layouts  4.7 us
  transfers between devices with their start and end apart: 38, of which 20 were waited for; matrix products, arithmetic and copies ran while one was open for 12% of the time, Pallas kernels for 0%

profile of v1, /device:TPU:0, one launch (start us, length us, event | category | flops | bytes accessed | tf_op | source)
XLA Modules:
  0.0 167.4 jit_solution(9825204864959209741)
XLA Ops:
  2.7 6.0 %collective-permute-start.17 = (bf16[1,24,896]{2,1,0:T(8,128)(2,1)S(1)}, bf16[1,24,896]{2,1,0:T(8,128)(2,1)S(1)}, u32[]{:S(2)}, u32[]{:S(2)}) collective-permute-start(bf16[1,24,896]{2,1,0:T(8,128)(2,1)S(1)} %get-tuple-element.58), channel_id=1, source_target_pairs={{0,7},{1,6},{2,5},{3,4},{4,3},{5,2},{6,1},{7,0},{8,15},{9,14},{10,... | collective-permute-start | bytes 129032 | tf_op jit(solution)/shard_map/ppermute | solution.py:109
  17.1 3.0 %collective-permute-done.12 = bf16[1,24,896]{2,1,0:T(8,128)(2,1)S(1)} collective-permute-done((bf16[1,24,896]{2,1,0:T(8,128)(2,1)S(1)}, bf16[1,24,896]{2,1,0:T(8,128)(2,1)S(1)}, u32[]{:S(2)}, u32[]{:S(2)}) %collective-permute-start.12) | collective-permute-done | bytes 43040 | tf_op jit(solution)/shard_map/ppermute | solution.py:109
  22.5 2.6 %collective-permute-done.13 = bf16[1,24,896]{2,1,0:T(8,128)(2,1)S(1)} collective-permute-done((bf16[1,24,896]{2,1,0:T(8,128)(2,1)S(1)}, bf16[1,24,896]{2,1,0:T(8,128)(2,1)S(1)}, u32[]{:S(2)}, u32[]{:S(2)}) %collective-permute-start.13) | collective-permute-done | bytes 43040 | tf_op jit(solution)/shard_map/ppermute | solution.py:109
  25.0 4.6 %collective-permute-start.6 = (bf16[1,24,1024]{2,1,0:T(8,128)(2,1)S(1)}, bf16[1,24,1024]{2,1,0:T(8,128)(2,1)S(1)}, u32[]{:S(2)}, u32[]{:S(2)}) collective-permute-start(bf16[1,24,1024]{2,1,0:T(8,128)(2,1)S(1)} %get-tuple-element.42), channel_id=1, source_target_pairs={{0,7},{1,6},{2,5},{3,4},{4,3},{5,2},{6,1},{7,0},{8,15},{9,14},{10,... | collective-permute-start | bytes 147464 | tf_op jit(solution)/shard_map/ppermute | solution.py:109
  34.5 2.5 %collective-permute-done = bf16[1,24,1024]{2,1,0:T(8,128)(2,1)S(1)} collective-permute-done((bf16[1,24,1024]{2,1,0:T(8,128)(2,1)S(1)}, bf16[1,24,1024]{2,1,0:T(8,128)(2,1)S(1)}, u32[]{:S(2)}, u32[]{:S(2)}) %collective-permute-start) | collective-permute-done | bytes 49184 | tf_op jit(solution)/shard_map/ppermute | solution.py:109
  38.5 2.7 %collective-permute-done.1 = bf16[1,24,1024]{2,1,0:T(8,128)(2,1)S(1)} collective-permute-done((bf16[1,24,1024]{2,1,0:T(8,128)(2,1)S(1)}, bf16[1,24,1024]{2,1,0:T(8,128)(2,1)S(1)}, u32[]{:S(2)}, u32[]{:S(2)}) %collective-permute-start.1) | collective-permute-done | bytes 49184 | tf_op jit(solution)/shard_map/ppermute | solution.py:109
  43.5 2.7 %collective-permute-done.2 = bf16[1,24,1024]{2,1,0:T(8,128)(2,1)S(1)} collective-permute-done((bf16[1,24,1024]{2,1,0:T(8,128)(2,1)S(1)}, bf16[1,24,1024]{2,1,0:T(8,128)(2,1)S(1)}, u32[]{:S(2)}, u32[]{:S(2)}) %collective-permute-start.2) | collective-permute-done | bytes 49184 | tf_op jit(solution)/shard_map/ppermute | solution.py:109
  47.8 5.6 %collective-permute-done.18 = bf16[1,192,896]{2,1,0:T(8,128)(2,1)S(1)} collective-permute-done((bf16[1,192,896]{2,1,0:T(8,128)(2,1)S(1)}, bf16[1,192,896]{2,1,0:T(8,128)(2,1)S(1)}, u32[]{:S(2)}, u32[]{:S(2)}) %collective-permute-start.18) | collective-permute-done | bytes 344096 | tf_op jit(solution)/shard_map/ppermute | solution.py:44
  56.4 8.6 %collective-permute-done.7 = bf16[1,192,896]{2,1,0:T(8,128)(2,1)S(1)} collective-permute-done((bf16[1,192,896]{2,1,0:T(8,128)(2,1)S(1)}, bf16[1,192,896]{2,1,0:T(8,128)(2,1)S(1)}, u32[]{:S(2)}, u32[]{:S(2)}) %collective-permute-start.7) | collective-permute-done | bytes 344096 | tf_op jit(solution)/shard_map/ppermute | solution.py:44
  77.7 3.0 %convolution_convert_fusion = bf16[4,896,512]{2,1,0:T(8,128)(2,1)} fusion(bf16[4,192,896]{2,1,0:T(8,128)(2,1)S(1)} %bitcast.160, bf16[192,512,1]{1,0,2:T(8,128)(2,1)S(1)} %get-tuple-element.29), kind=kOutput, calls=%fused_computation.4 | convolution fusion | flops 706478080 | bytes 5242880 | tf_op jit(solution)/shard_map/nsd,sf->ndf/dot_general | solution.py:171
  83.1 3.0 %convolution_convert_fusion.1 = bf16[4,896,512]{2,1,0:T(8,128)(2,1)} fusion(bf16[4,192,896]{2,1,0:T(8,128)(2,1)S(1)} %bitcast.161, bf16[192,512]{1,0:T(8,128)(2,1)S(1)} %get-tuple-element.30), kind=kOutput, calls=%fused_computation.5 | convolution fusion | flops 706478080 | bytes 5242880 | tf_op jit(solution)/shard_map/nsd,sf->ndf/dot_general | solution.py:166
  95.5 7.5 %collective-permute-done.30 = bf16[1,192,896]{2,1,0:T(8,128)(2,1)S(1)} collective-permute-done((bf16[1,192,896]{2,1,0:T(8,128)(2,1)S(1)}, bf16[1,192,896]{2,1,0:T(8,128)(2,1)S(1)}, u32[]{:S(2)}, u32[]{:S(2)}) %collective-permute-start.30) | collective-permute-done | bytes 344096 | tf_op jit(solution)/shard_map/ppermute | solution.py:60
  104.8 4.1 %collective-permute-done.10 = bf16[1,192,896]{2,1,0:T(8,128)(2,1)S(1)} collective-permute-done((bf16[1,192,896]{2,1,0:T(8,128)(2,1)S(1)}, bf16[1,192,896]{2,1,0:T(8,128)(2,1)S(1)}, u32[]{:S(2)}, u32[]{:S(2)}) %collective-permute-start.10) | collective-permute-done | bytes 344096 | tf_op jit(solution)/shard_map/ppermute | solution.py:60
  109.2 5.2 %collective-permute-start.28 = (bf16[1,24,1024]{2,1,0:T(8,128)(2,1)S(1)}, bf16[1,24,1024]{2,1,0:T(8,128)(2,1)S(1)}, u32[]{:S(2)}, u32[]{:S(2)}) collective-permute-start(bf16[1,24,1024]{2,1,0:T(8,128)(2,1)S(1)} %get-tuple-element.32), channel_id=1, source_target_pairs={{0,7},{1,6},{2,5},{3,4},{4,3},{5,2},{6,1},{7,0},{8,15},{9,14},{10,... | collective-permute-start | bytes 147464 | tf_op jit(solution)/shard_map/ppermute | solution.py:109
  118.8 3.2 %collective-permute-done.32 = bf16[1,24,896]{2,1,0:T(8,128)(2,1)S(1)} collective-permute-done((bf16[1,24,896]{2,1,0:T(8,128)(2,1)S(1)}, bf16[1,24,896]{2,1,0:T(8,128)(2,1)S(1)}, u32[]{:S(2)}, u32[]{:S(2)}) %collective-permute-start.32) | collective-permute-done | bytes 43040 | tf_op jit(solution)/shard_map/ppermute | solution.py:109
  123.8 3.0 %collective-permute-done.33 = bf16[1,24,896]{2,1,0:T(8,128)(2,1)S(1)} collective-permute-done((bf16[1,24,896]{2,1,0:T(8,128)(2,1)S(1)}, bf16[1,24,896]{2,1,0:T(8,128)(2,1)S(1)}, u32[]{:S(2)}, u32[]{:S(2)}) %collective-permute-start.33) | collective-permute-done | bytes 43040 | tf_op jit(solution)/shard_map/ppermute | solution.py:109
  129.1 3.9 %collective-permute-done.34 = bf16[1,24,896]{2,1,0:T(8,128)(2,1)S(1)} collective-permute-done((bf16[1,24,896]{2,1,0:T(8,128)(2,1)S(1)}, bf16[1,24,896]{2,1,0:T(8,128)(2,1)S(1)}, u32[]{:S(2)}, u32[]{:S(2)}) %collective-permute-start.34) | collective-permute-done | bytes 43040 | tf_op jit(solution)/shard_map/ppermute | solution.py:109
  135.5 4.3 %collective-permute-done.35 = bf16[1,24,896]{2,1,0:T(8,128)(2,1)S(1)} collective-permute-done((bf16[1,24,896]{2,1,0:T(8,128)(2,1)S(1)}, bf16[1,24,896]{2,1,0:T(8,128)(2,1)S(1)}, u32[]{:S(2)}, u32[]{:S(2)}) %collective-permute-start.35) | collective-permute-done | bytes 43040 | tf_op jit(solution)/shard_map/ppermute | solution.py:109
  142.3 3.3 %collective-permute-done.36 = bf16[1,24,896]{2,1,0:T(8,128)(2,1)S(1)} collective-permute-done((bf16[1,24,896]{2,1,0:T(8,128)(2,1)S(1)}, bf16[1,24,896]{2,1,0:T(8,128)(2,1)S(1)}, u32[]{:S(2)}, u32[]{:S(2)}) %collective-permute-start.36) | collective-permute-done | bytes 43040 | tf_op jit(solution)/shard_map/ppermute | solution.py:109
  145.6 3.1 %collective-permute-start.37 = (bf16[1,24,896]{2,1,0:T(8,128)(2,1)S(1)}, bf16[1,24,896]{2,1,0:T(8,128)(2,1)S(1)}, u32[]{:S(2)}, u32[]{:S(2)}) collective-permute-start(bf16[1,24,896]{2,1,0:T(8,128)(2,1)S(1)} %get-tuple-element.50), channel_id=1, source_target_pairs={{0,7},{1,6},{2,5},{3,4},{4,3},{5,2},{6,1},{7,0},{8,15},{9,14},{10,... | collective-permute-start | bytes 129032 | tf_op jit(solution)/shard_map/ppermute | solution.py:109
  148.7 3.6 %collective-permute-done.37 = bf16[1,24,896]{2,1,0:T(8,128)(2,1)S(1)} collective-permute-done((bf16[1,24,896]{2,1,0:T(8,128)(2,1)S(1)}, bf16[1,24,896]{2,1,0:T(8,128)(2,1)S(1)}, u32[]{:S(2)}, u32[]{:S(2)}) %collective-permute-start.37) | collective-permute-done | bytes 43040 | tf_op jit(solution)/shard_map/ppermute | solution.py:109
  153.8 2.7 %collective-permute-done.22 = bf16[1,24,1024]{2,1,0:T(8,128)(2,1)S(1)} collective-permute-done((bf16[1,24,1024]{2,1,0:T(8,128)(2,1)S(1)}, bf16[1,24,1024]{2,1,0:T(8,128)(2,1)S(1)}, u32[]{:S(2)}, u32[]{:S(2)}) %collective-permute-start.22) | collective-permute-done | bytes 49184 | tf_op jit(solution)/shard_map/ppermute | solution.py:109
  156.5 4.1 %collective-permute-done.23 = bf16[1,24,1024]{2,1,0:T(8,128)(2,1)S(1)} collective-permute-done((bf16[1,24,1024]{2,1,0:T(8,128)(2,1)S(1)}, bf16[1,24,1024]{2,1,0:T(8,128)(2,1)S(1)}, u32[]{:S(2)}, u32[]{:S(2)}) %collective-permute-start.23) | collective-permute-done | bytes 49184 | tf_op jit(solution)/shard_map/ppermute | solution.py:109
  160.6 5.0 %collective-permute-done.24 = bf16[1,24,1024]{2,1,0:T(8,128)(2,1)S(1)} collective-permute-done((bf16[1,24,1024]{2,1,0:T(8,128)(2,1)S(1)}, bf16[1,24,1024]{2,1,0:T(8,128)(2,1)S(1)}, u32[]{:S(2)}, u32[]{:S(2)}) %collective-permute-start.24) | collective-permute-done | bytes 49184 | tf_op jit(solution)/shard_map/ppermute | solution.py:109
  (159 shorter events, 69.0 us)
Async XLA Ops:
  2.7 30.3 %collective-permute-start.17 = (bf16[1,24,896]{2,1,0:T(8,128)(2,1)S(1)}, bf16[1,24,896]{2,1,0:T(8,128)(2,1)S(1)}, u32[]{:S(2)}, u32[]{:S(2)}) collective-permute-start(bf16[1,24,896]{2,1,0:T(8,128)(2,1)S(1)} %get-tuple-element.58), channel_id=1, source_target_pairs={{0,7},{1,6},{2,5},{3,4},{4,3},{5,2},{6,1},{7,0},{8,15},{9,14},{10,... | collective-permute-start | bytes 129032 | tf_op jit(solution)/shard_map/ppermute | solution.py:109
  8.7 22.1 %collective-permute-start.16 = (bf16[1,24,896]{2,1,0:T(8,128)(2,1)S(1)}, bf16[1,24,896]{2,1,0:T(8,128)(2,1)S(1)}, u32[]{:S(2)}, u32[]{:S(2)}) collective-permute-start(bf16[1,24,896]{2,1,0:T(8,128)(2,1)S(1)} %get-tuple-element.59), channel_id=1, source_target_pairs={{0,6},{1,7},{2,4},{3,5},{4,2},{5,3},{6,0},{7,1},{8,14},{9,15},{10,... | collective-permute-start | bytes 129032 | tf_op jit(solution)/shard_map/ppermute | solution.py:109
  8.9 21.0 %collective-permute-start.15 = (bf16[1,24,896]{2,1,0:T(8,128)(2,1)S(1)}, bf16[1,24,896]{2,1,0:T(8,128)(2,1)S(1)}, u32[]{:S(2)}, u32[]{:S(2)}) collective-permute-start(bf16[1,24,896]{2,1,0:T(8,128)(2,1)S(1)} %get-tuple-element.60), channel_id=1, source_target_pairs={{0,5},{1,4},{2,7},{3,6},{4,1},{5,0},{6,3},{7,2},{8,13},{9,12},{10,... | collective-permute-start | bytes 129032 | tf_op jit(solution)/shard_map/ppermute | solution.py:109
  9.7 20.0 %collective-permute-start.14 = (bf16[1,24,896]{2,1,0:T(8,128)(2,1)S(1)}, bf16[1,24,896]{2,1,0:T(8,128)(2,1)S(1)}, u32[]{:S(2)}, u32[]{:S(2)}) collective-permute-start(bf16[1,24,896]{2,1,0:T(8,128)(2,1)S(1)} %get-tuple-element.61), channel_id=1, source_target_pairs={{0,4},{1,5},{2,6},{3,7},{4,0},{5,1},{6,2},{7,3},{8,12},{9,13},{10,... | collective-permute-start | bytes 129032 | tf_op jit(solution)/shard_map/ppermute | solution.py:109
  25.0 22.8 %collective-permute-start.6 = (bf16[1,24,1024]{2,1,0:T(8,128)(2,1)S(1)}, bf16[1,24,1024]{2,1,0:T(8,128)(2,1)S(1)}, u32[]{:S(2)}, u32[]{:S(2)}) collective-permute-start(bf16[1,24,1024]{2,1,0:T(8,128)(2,1)S(1)} %get-tuple-element.42), channel_id=1, source_target_pairs={{0,7},{1,6},{2,5},{3,4},{4,3},{5,2},{6,1},{7,0},{8,15},{9,14},{10,... | collective-permute-start | bytes 147464 | tf_op jit(solution)/shard_map/ppermute | solution.py:109
  29.6 18.1 %collective-permute-start.5 = (bf16[1,24,1024]{2,1,0:T(8,128)(2,1)S(1)}, bf16[1,24,1024]{2,1,0:T(8,128)(2,1)S(1)}, u32[]{:S(2)}, u32[]{:S(2)}) collective-permute-start(bf16[1,24,1024]{2,1,0:T(8,128)(2,1)S(1)} %get-tuple-element.43), channel_id=1, source_target_pairs={{0,6},{1,7},{2,4},{3,5},{4,2},{5,3},{6,0},{7,1},{8,14},{9,15},{10,... | collective-permute-start | bytes 147464 | tf_op jit(solution)/shard_map/ppermute | solution.py:109
  29.9 17.8 %collective-permute-start.4 = (bf16[1,24,1024]{2,1,0:T(8,128)(2,1)S(1)}, bf16[1,24,1024]{2,1,0:T(8,128)(2,1)S(1)}, u32[]{:S(2)}, u32[]{:S(2)}) collective-permute-start(bf16[1,24,1024]{2,1,0:T(8,128)(2,1)S(1)} %get-tuple-element.44), channel_id=1, source_target_pairs={{0,5},{1,4},{2,7},{3,6},{4,1},{5,0},{6,3},{7,2},{8,13},{9,12},{10,... | collective-permute-start | bytes 147464 | tf_op jit(solution)/shard_map/ppermute | solution.py:109
  30.8 16.9 %collective-permute-start.3 = (bf16[1,24,1024]{2,1,0:T(8,128)(2,1)S(1)}, bf16[1,24,1024]{2,1,0:T(8,128)(2,1)S(1)}, u32[]{:S(2)}, u32[]{:S(2)}) collective-permute-start(bf16[1,24,1024]{2,1,0:T(8,128)(2,1)S(1)} %get-tuple-element.45), channel_id=1, source_target_pairs={{0,4},{1,5},{2,6},{3,7},{4,0},{5,1},{6,2},{7,3},{8,12},{9,13},{10,... | collective-permute-start | bytes 147464 | tf_op jit(solution)/shard_map/ppermute | solution.py:109
  46.1 7.2 %collective-permute-start.18 = (bf16[1,192,896]{2,1,0:T(8,128)(2,1)S(1)}, bf16[1,192,896]{2,1,0:T(8,128)(2,1)S(1)}, u32[]{:S(2)}, u32[]{:S(2)}) collective-permute-start(bf16[1,192,896]{2,1,0:T(8,128)(2,1)S(1)} %bitcast.174), channel_id=1, source_target_pairs={{0,16},{8,24},{16,0},{24,8},{1,17},{9,25},{17,1},{25,9},{2,18},{10... | collective-permute-start | bytes 1032200 | tf_op jit(solution)/shard_map/ppermute | solution.py:44
  54.4 10.9 %collective-permute-start.19 = (bf16[2,192,896]{2,1,0:T(8,128)(2,1)}, bf16[2,192,896]{2,1,0:T(8,128)(2,1)S(1)}, u32[]{:S(2)}, u32[]{:S(2)}) collective-permute-start(bf16[2,192,896]{2,1,0:T(8,128)(2,1)} %maximum_select_fusion.4), channel_id=1, source_target_pairs={{0,8},{8,0},{16,24},{24,16},{1,9},{9,1},{17,25},{25,17},{2,10},{10... | collective-permute-start | bytes 2064392 | tf_op jit(solution)/shard_map/ppermute | solution.py:44
  54.4 10.5 %collective-permute-start.7 = (bf16[1,192,896]{2,1,0:T(8,128)(2,1)S(1)}, bf16[1,192,896]{2,1,0:T(8,128)(2,1)S(1)}, u32[]{:S(2)}, u32[]{:S(2)}) collective-permute-start(bf16[1,192,896]{2,1,0:T(8,128)(2,1)S(1)} %get-tuple-element.41), channel_id=1, source_target_pairs={{0,16},{8,24},{16,0},{24,8},{1,17},{9,25},{17,1},{25,9},{2,18},{10... | collective-permute-start | bytes 1032200 | tf_op jit(solution)/shard_map/ppermute | solution.py:44
  75.8 10.4 %collective-permute-start.20 = (f32[192]{0:T(256)S(1)}, f32[192]{0:T(256)S(1)}, u32[]{:S(2)}, u32[]{:S(2)}) collective-permute-start(f32[192]{0:T(256)S(1)} %get-tuple-element.25), channel_id=1, source_target_pairs={{0,8},{8,0},{16,24},{24,16},{1,9},{9,1},{17,25},{25,17},{2,10},{10... | collective-permute-start | bytes 2312 | tf_op jit(solution)/shard_map/ppermute | solution.py:67
  83.1 7.4 %collective-permute-start.29 = (bf16[2,192,896]{2,1,0:T(8,128)(2,1)}, bf16[2,192,896]{2,1,0:T(8,128)(2,1)}, u32[]{:S(2)}, u32[]{:S(2)}) collective-permute-start(bf16[2,192,896]{2,1,0:T(8,128)(2,1)} %fusion.18), channel_id=1, source_target_pairs={{0,8},{8,0},{16,24},{24,16},{1,9},{9,1},{17,25},{25,17},{2,10},{10... | collective-permute-start | bytes 2064392 | tf_op jit(solution)/shard_map/ppermute | solution.py:60
  91.9 11.1 %collective-permute-start.30 = (bf16[1,192,896]{2,1,0:T(8,128)(2,1)S(1)}, bf16[1,192,896]{2,1,0:T(8,128)(2,1)S(1)}, u32[]{:S(2)}, u32[]{:S(2)}) collective-permute-start(bf16[1,192,896]{2,1,0:T(8,128)(2,1)S(1)} %fusion.24), channel_id=1, source_target_pairs={{0,16},{8,24},{16,0},{24,8},{1,17},{9,25},{17,1},{25,9},{2,18},{10... | collective-permute-start | bytes 1032200 | tf_op jit(solution)/shard_map/ppermute | solution.py:60
  95.0 13.9 %collective-permute-start.10 = (bf16[1,192,896]{2,1,0:T(8,128)(2,1)S(1)}, bf16[1,192,896]{2,1,0:T(8,128)(2,1)S(1)}, u32[]{:S(2)}, u32[]{:S(2)}) collective-permute-start(bf16[1,192,896]{2,1,0:T(8,128)(2,1)S(1)} %fusion.23), channel_id=1, source_target_pairs={{0,16},{8,24},{16,0},{24,8},{1,17},{9,25},{17,1},{25,9},{2,18},{10... | collective-permute-start | bytes 1032200 | tf_op jit(solution)/shard_map/ppermute | solution.py:60
  103.2 14.2 %collective-permute-start.31 = (bf16[1,24,896]{2,1,0:T(8,128)(2,1)S(1)}, bf16[1,24,896]{2,1,0:T(8,128)(2,1)S(1)}, u32[]{:S(2)}, u32[]{:S(2)}) collective-permute-start(bf16[1,24,896]{2,1,0:T(8,128)(2,1)S(1)} %get-tuple-element.56), channel_id=1, source_target_pairs={{0,1},{1,0},{2,3},{3,2},{4,5},{5,4},{6,7},{7,6},{8,9},{9,8},{10,11... | collective-permute-start | bytes 129032 | tf_op jit(solution)/shard_map/ppermute | solution.py:109
  109.2 56.4 %collective-permute-start.28 = (bf16[1,24,1024]{2,1,0:T(8,128)(2,1)S(1)}, bf16[1,24,1024]{2,1,0:T(8,128)(2,1)S(1)}, u32[]{:S(2)}, u32[]{:S(2)}) collective-permute-start(bf16[1,24,1024]{2,1,0:T(8,128)(2,1)S(1)} %get-tuple-element.32), channel_id=1, source_target_pairs={{0,7},{1,6},{2,5},{3,4},{4,3},{5,2},{6,1},{7,0},{8,15},{9,14},{10,... | collective-permute-start | bytes 147464 | tf_op jit(solution)/shard_map/ppermute | solution.py:109
  114.4 51.2 %collective-permute-start.27 = (bf16[1,24,1024]{2,1,0:T(8,128)(2,1)S(1)}, bf16[1,24,1024]{2,1,0:T(8,128)(2,1)S(1)}, u32[]{:S(2)}, u32[]{:S(2)}) collective-permute-start(bf16[1,24,1024]{2,1,0:T(8,128)(2,1)S(1)} %get-tuple-element.33), channel_id=1, source_target_pairs={{0,6},{1,7},{2,4},{3,5},{4,2},{5,3},{6,0},{7,1},{8,14},{9,15},{10,... | collective-permute-start | bytes 147464 | tf_op jit(solution)/shard_map/ppermute | solution.py:109
  114.4 51.2 %collective-permute-start.26 = (bf16[1,24,1024]{2,1,0:T(8,128)(2,1)S(1)}, bf16[1,24,1024]{2,1,0:T(8,128)(2,1)S(1)}, u32[]{:S(2)}, u32[]{:S(2)}) collective-permute-start(bf16[1,24,1024]{2,1,0:T(8,128)(2,1)S(1)} %get-tuple-element.34), channel_id=1, source_target_pairs={{0,5},{1,4},{2,7},{3,6},{4,1},{5,0},{6,3},{7,2},{8,13},{9,12},{10,... | collective-permute-start | bytes 147464 | tf_op jit(solution)/shard_map/ppermute | solution.py:109
  114.9 50.6 %collective-permute-start.25 = (bf16[1,24,1024]{2,1,0:T(8,128)(2,1)S(1)}, bf16[1,24,1024]{2,1,0:T(8,128)(2,1)S(1)}, u32[]{:S(2)}, u32[]{:S(2)}) collective-permute-start(bf16[1,24,1024]{2,1,0:T(8,128)(2,1)S(1)} %get-tuple-element.35), channel_id=1, source_target_pairs={{0,4},{1,5},{2,6},{3,7},{4,0},{5,1},{6,2},{7,3},{8,12},{9,13},{10,... | collective-permute-start | bytes 147464 | tf_op jit(solution)/shard_map/ppermute | solution.py:109
  126.9 6.2 %collective-permute-start.34 = (bf16[1,24,896]{2,1,0:T(8,128)(2,1)S(1)}, bf16[1,24,896]{2,1,0:T(8,128)(2,1)S(1)}, u32[]{:S(2)}, u32[]{:S(2)}) collective-permute-start(bf16[1,24,896]{2,1,0:T(8,128)(2,1)S(1)} %get-tuple-element.53), channel_id=1, source_target_pairs={{0,4},{1,5},{2,6},{3,7},{4,0},{5,1},{6,2},{7,3},{8,12},{9,13},{10,... | collective-permute-start | bytes 129032 | tf_op jit(solution)/shard_map/ppermute | solution.py:109
  133.1 6.8 %collective-permute-start.35 = (bf16[1,24,896]{2,1,0:T(8,128)(2,1)S(1)}, bf16[1,24,896]{2,1,0:T(8,128)(2,1)S(1)}, u32[]{:S(2)}, u32[]{:S(2)}) collective-permute-start(bf16[1,24,896]{2,1,0:T(8,128)(2,1)S(1)} %get-tuple-element.52), channel_id=1, source_target_pairs={{0,5},{1,4},{2,7},{3,6},{4,1},{5,0},{6,3},{7,2},{8,13},{9,12},{10,... | collective-permute-start | bytes 129032 | tf_op jit(solution)/shard_map/ppermute | solution.py:109
  139.8 5.8 %collective-permute-start.36 = (bf16[1,24,896]{2,1,0:T(8,128)(2,1)S(1)}, bf16[1,24,896]{2,1,0:T(8,128)(2,1)S(1)}, u32[]{:S(2)}, u32[]{:S(2)}) collective-permute-start(bf16[1,24,896]{2,1,0:T(8,128)(2,1)S(1)} %get-tuple-element.51), channel_id=1, source_target_pairs={{0,6},{1,7},{2,4},{3,5},{4,2},{5,3},{6,0},{7,1},{8,14},{9,15},{10,... | collective-permute-start | bytes 129032 | tf_op jit(solution)/shard_map/ppermute | solution.py:109
  145.6 6.7 %collective-permute-start.37 = (bf16[1,24,896]{2,1,0:T(8,128)(2,1)S(1)}, bf16[1,24,896]{2,1,0:T(8,128)(2,1)S(1)}, u32[]{:S(2)}, u32[]{:S(2)}) collective-permute-start(bf16[1,24,896]{2,1,0:T(8,128)(2,1)S(1)} %get-tuple-element.50), channel_id=1, source_target_pairs={{0,7},{1,6},{2,5},{3,4},{4,3},{5,2},{6,1},{7,0},{8,15},{9,14},{10,... | collective-permute-start | bytes 129032 | tf_op jit(solution)/shard_map/ppermute | solution.py:109
  (22 other events, 99.6 us)
